TPU v7x, 256 devices: a whole 4x4x8 slice. The times are simulated.
256 devices in a mesh: group: 8 (over y, core), dev: 32 (over x, z).
Axes of the slice: x: 4, y: 4, z: 8, core: 2. Of those that a mesh axis runs over, the one named last changes fastest.
Arguments:
- embeddings: bfloat16 [262144, 768], P(('group', 'dev')), may hold values from -6 to 6
- cluster_ids: int32 [1024], P(('group', 'dev')), may hold values from 0 to 1023, as said below
Outputs:
- nearest: float32 [262144], P(('group', 'dev'))
Inputs may be any that keep to these rules, and one draw needn't show every extreme that they name: `cluster_ids`: each cluster is a run of 1 to 29 consecutive blocks inside one cluster group of 128 blocks (a group's first block starts a cluster, its last block is a cluster of one block), and its id is the index of its first block; some cluster of every group has exactly 29 blocks.
All inputs are finite; a program needn't handle non-finite values.
Results may differ from a plain program's by a relative error of at most 0.0012.
Values may be sent and summed in bfloat16 or wider, within the bound.
No kernel may reach another device: no remote copies, remote signals or barrier semaphores. Data moves between devices by JAX's collectives and lax.ppermute only.
A program may use at most 192 MiB of HBM per device.

v0:
```python
import jax
import jax.numpy as jnp
from jax import lax
from jax.sharding import PartitionSpec as P


def from_behind(value, axis, steps):
    count = lax.axis_size(axis)
    initial, last = (max(0, -steps), min(count, count - steps))
    return lax.ppermute(value, axis, [(source, source + steps) for source in range(initial, last)])


def unit_rows(embeddings):
    values_f = embeddings.astype(jnp.float32)
    squares = jnp.sum(values_f * values_f, axis=1, keepdims=True)
    return (values_f * lax.rsqrt(squares + 1e-06)).astype(jnp.bfloat16)


def body(embeddings, cluster_ids):
    rows, dim = embeddings.shape
    blocks = cluster_ids.shape[0]
    width = rows // blocks
    half = blocks // 2
    count = lax.axis_size("dev")
    place = lax.axis_index("dev")
    first_block = (lax.axis_index("group") * count + place) * blocks
    unit = unit_rows(embeddings)

    own_tags = jnp.repeat(cluster_ids, width)
    local = jnp.arange(rows, dtype=jnp.int32)
    scores = jnp.dot(unit, unit.T, preferred_element_type=jnp.float32)
    keep = (own_tags[:, None] == own_tags[None, :]) & (local[:, None] != local[None, :])
    best = jnp.max(jnp.where(keep, scores + 2.0, jnp.zeros_like(scores)), axis=1)

    lag = first_block + jnp.arange(blocks, dtype=jnp.int32) - cluster_ids
    meta = jnp.zeros((16, dim), jnp.bfloat16).at[0, :blocks].set(lag.astype(jnp.bfloat16))
    packet = jnp.concatenate([unit, meta], axis=0)

    ahead = [packet]
    for step in range(3):
        ahead.append(from_behind(ahead[-1], "dev", -1))
    ahead.append(from_behind(jnp.concatenate([ahead[3][: half * width], ahead[3][rows:]], axis=0), "dev", -1))
    behind = [unit]
    for step in range(3):
        behind.append(from_behind(behind[-1], "dev", 1))
    behind.append(from_behind(behind[3][half * width:], "dev", 1))

    def tile(i, a_blocks, j, b_count):
        a = behind[i]
        b = ahead[j]
        b_lag = b[b_count * width, :b_count].astype(jnp.int32)
        block_reach = (i + j) * blocks + jnp.arange(b_count, dtype=jnp.int32) - b_lag
        a_rows = jnp.repeat(jnp.array(a_blocks, jnp.int32), width)
        b_rows = jnp.concatenate(
            [jnp.repeat(block_reach, width), jnp.full((b.shape[0] - b_count * width,), rows, jnp.int32)]
        )
        matched = (jnp.min(block_reach) <= a_blocks[-1]) & (place >= i)

        def compute(unused):
            sims = jnp.dot(a, b.T, preferred_element_type=jnp.float32)
            same = b_rows[None, :] <= a_rows[:, None]
            shifted = jnp.where(same, sims + 2.0, jnp.zeros_like(sims))
            return jnp.max(shifted, axis=1), jnp.max(shifted, axis=0)[: b_count * width]

        def skipped(unused):
            return (jnp.zeros((a.shape[0],), jnp.float32), jnp.zeros((b_count * width,), jnp.float32))

        return lax.cond(matched, compute, skipped, 0)

    everything = list(range(blocks))
    plan = [(k // 2, everything, k - k // 2, blocks) for k in range(1, 7)]
    plan += [(3, everything, 4, half), (4, everything[half:], 3, blocks)]
    to_ahead = {}
    to_behind = {}
    for i, a_blocks, j, b_count in plan:
        row_part, column_part = tile(i, a_blocks, j, b_count)
        if i == 0:
            best = jnp.maximum(best, row_part)
        else:
            to_behind[i] = jnp.maximum(to_behind[i], row_part) if i in to_behind else row_part
        to_ahead[j] = jnp.maximum(to_ahead[j], column_part) if j in to_ahead else column_part

    for i, part in to_behind.items():
        arrived = from_behind(part, "dev", -i)
        best = best.at[rows - part.shape[0]:].max(arrived)
    for j, part in to_ahead.items():
        arrived = from_behind(part, "dev", j)
        best = best.at[: part.shape[0]].max(arrived)
    return best - 2.0


def solution(mesh):
    return jax.shard_map(
        body,
        mesh=mesh,
        in_specs=(P(("group", "dev"), None), P(("group", "dev"))),
        out_specs=P(("group", "dev")),
        check_vma=False,
    )
```

profile of v0, /device:TPU:4, one launch (start us, length us, event | category | flops | bytes accessed | tf_op | source)
XLA Modules:
  0.0 209.2 jit_solution(4857587988262376479)
XLA Ops:
  0.0 1.9 fusion.11
  1.9 0.0 copy-start.4
  1.9 0.3 fusion.12
  2.3 0.3 copy-done.4
  2.6 0.1 fusion.13
  2.7 7.7 %collective-permute-start = (bf16[1040,768]{1,0:T(8,128)(2,1)S(1)}, bf16[1040,768]{1,0:T(8,128)(2,1)}, u32[]{:S(2)}, u32[]{:S(2)}) collective-permute-start(bf16[1040,768]{1,0:T(8,128)(2,1)S(1)} %fusion.13), channel_id=1, source_target_pairs={{1,0},{2,1},{3,2},{4,3},{5,4},{6,5},{7,6},{8,7},{9,8},{10,9},{11,1... | collective-permute-start | bytes 4792328 | tf_op jit(solution)/shard_map/ppermute | solution.py:10
  10.4 1.9 collective-permute-start.1
  12.4 32.2 %collective-permute-done = bf16[1040,768]{1,0:T(8,128)(2,1)} collective-permute-done((bf16[1040,768]{1,0:T(8,128)(2,1)S(1)}, bf16[1040,768]{1,0:T(8,128)(2,1)}, u32[]{:S(2)}, u32[]{:S(2)}) %collective-permute-start) | collective-permute-done | bytes 1597472 | tf_op jit(solution)/shard_map/ppermute | solution.py:10
  44.6 6.6 %collective-permute-start.2 = (bf16[1040,768]{1,0:T(8,128)(2,1)}, bf16[1040,768]{1,0:T(8,128)(2,1)}, u32[]{:S(2)}, u32[]{:S(2)}) collective-permute-start(bf16[1040,768]{1,0:T(8,128)(2,1)} %collective-permute-done), channel_id=1, source_target_pairs={{1,0},{2,1},{3,2},{4,3},{5,4},{6,5},{7,6},{8,7},{9,8},{10,9},{11,1... | collective-permute-start | bytes 4792328 | tf_op jit(solution)/shard_map/ppermute | solution.py:10
  51.2 1.9 collective-permute-start.4
  53.1 31.7 %collective-permute-done.2 = bf16[1040,768]{1,0:T(8,128)(2,1)} collective-permute-done((bf16[1040,768]{1,0:T(8,128)(2,1)}, bf16[1040,768]{1,0:T(8,128)(2,1)}, u32[]{:S(2)}, u32[]{:S(2)}) %collective-permute-start.2) | collective-permute-done | bytes 1597472 | tf_op jit(solution)/shard_map/ppermute | solution.py:10
  84.8 6.5 %collective-permute-start.5 = (bf16[1040,768]{1,0:T(8,128)(2,1)}, bf16[1040,768]{1,0:T(8,128)(2,1)S(1)}, u32[]{:S(2)}, u32[]{:S(2)}) collective-permute-start(bf16[1040,768]{1,0:T(8,128)(2,1)} %collective-permute-done.2), channel_id=1, source_target_pairs={{1,0},{2,1},{3,2},{4,3},{5,4},{6,5},{7,6},{8,7},{9,8},{10,9},{11,1... | collective-permute-start | bytes 4792328 | tf_op jit(solution)/shard_map/ppermute | solution.py:10
  91.3 0.0 collective-permute-done.4
  91.3 1.9 collective-permute-start.7
  93.2 0.1 broadcast_bitcast_fusion.16
  93.3 36.4 %collective-permute-done.7 = bf16[1024,768]{1,0:T(8,128)(2,1)S(1)} collective-permute-done((bf16[1024,768]{1,0:T(8,128)(2,1)}, bf16[1024,768]{1,0:T(8,128)(2,1)S(1)}, u32[]{:S(2)}, u32[]{:S(2)}) %collective-permute-start.7) | collective-permute-done | bytes 1572896 | tf_op jit(solution)/shard_map/ppermute | solution.py:10
  129.7 1.0 slice.170
  130.7 1.9 collective-permute-start.10
  132.6 0.0 collective-permute-done.5
  132.7 1.1 copy-done.1
  133.8 0.1 slice.167
  133.8 0.1 pad_maximum_fusion
  133.9 6.0 %collective-permute-start.8 = (bf16[528,768]{1,0:T(8,128)(2,1)S(1)}, bf16[528,768]{1,0:T(8,128)(2,1)}, u32[]{:S(2)}, u32[]{:S(2)}) collective-permute-start(bf16[528,768]{1,0:T(8,128)(2,1)S(1)} %pad_maximum_fusion), channel_id=1, source_target_pairs={{1,0},{2,1},{3,2},{4,3},{5,4},{6,5},{7,6},{8,7},{9,8},{10,9},{11,1... | collective-permute-start | bytes 2433032 | tf_op jit(solution)/shard_map/ppermute | solution.py:10
  140.0 2.1 select_reduce_fusion
  142.0 1.4 fusion.19
  144.7 3.6 %conditional.8 = (f32[1024]{0:T(1024)S(1)}, f32[1024]{0:T(1024)S(1)}) conditional(s32[]{:T(128)} %convert_element_type.66, () %tuple.123, (s32[4]{0:T(128)S(1)}, s32[4]{0:T(128)S(1)}, bf16[1024,768]{1,0:T(8,128)(2,1)S(1)}, bf16[1040,768]{1,0:T(8,128)(2,1)}) %tuple.124), branch_computations={%region_3.4_spmd, %region_4.7_spmd} | conditional | flops 1641101312 | bytes 3227892 | solution.py:68
  144.7 0.1 broadcast_bitcast_fusion
  144.8 3.5 %fusion.27 = (f32[1040]{0:T(1024)S(1)}, f32[1024]{0:T(1024)S(1)}) fusion(bf16[1024,768]{1,0:T(8,128)(2,1)S(1)} %get-tuple-element.267, bf16[1040,768]{1,0:T(8,128)(2,1)} %get-tuple-element.268, s32[1024]{0:T(1024)S(1)} %bitcast.132, s32[1040]{0:T(1024)S(1)} %concatenate.38), kind=kOutput, calls=%fused_computation.77 | convolution fusion | flops 1641101312 | bytes 3186816 | tf_op jit(solution)/shard_map/cond/branch_1_fun/dot_general | solution.py:60
  148.3 4.1 %conditional.9 = (f32[1024]{0:T(1024)S(1)}, f32[1024]{0:T(1024)S(1)}) conditional(s32[]{:T(128)} %convert_element_type.67, () %tuple.125, (s32[4]{0:T(128)S(1)}, s32[4]{0:T(128)S(1)}, bf16[1024,768]{1,0:T(8,128)(2,1)}, bf16[1040,768]{1,0:T(8,128)(2,1)}) %tuple.189), branch_computations={%region_8.9_spmd, %region_9.0_spmd} | conditional | flops 1641101312 | bytes 3227892 | solution.py:68
  148.3 0.1 broadcast_bitcast_fusion.2
  148.4 4.0 %fusion.28 = (f32[1040]{0:T(1024)S(1)}, f32[1024]{0:T(1024)S(1)}) fusion(bf16[1024,768]{1,0:T(8,128)(2,1)} %get-tuple-element.271, bf16[1040,768]{1,0:T(8,128)(2,1)} %get-tuple-element.272, s32[1024]{0:T(1024)S(1)} %bitcast.133, s32[1040]{0:T(1024)S(1)} %concatenate.39), kind=kOutput, calls=%fused_computation.78 | convolution fusion | flops 1641101312 | bytes 3186816 | tf_op jit(solution)/shard_map/cond/branch_1_fun/dot_general | solution.py:60
  152.4 1.9 collective-permute-start.12
  154.3 1.3 fusion.22
  156.9 2.4 %collective-permute-start.13 = (f32[1024]{0:T(1024)S(1)}, f32[1024]{0:T(1024)S(1)}, u32[]{:S(2)}, u32[]{:S(2)}) collective-permute-start(f32[1024]{0:T(1024)S(1)} %max.80), channel_id=1, source_target_pairs={{0,2},{1,3},{2,4},{3,5},{4,6},{5,7},{6,8},{7,9},{8,10},{9,11},{10,... | collective-permute-start | bytes 12296 | tf_op jit(solution)/shard_map/ppermute | solution.py:10
  159.3 13.7 %collective-permute-start.3 = (f32[1024]{0:T(1024)S(1)}, f32[1024]{0:T(1024)S(1)}, u32[]{:S(2)}, u32[]{:S(2)}) collective-permute-start(f32[1024]{0:T(1024)S(1)} %max.71), channel_id=1, source_target_pairs={{1,0},{2,1},{3,2},{4,3},{5,4},{6,5},{7,6},{8,7},{9,8},{10,9},{11,1... | collective-permute-start | bytes 12296 | tf_op jit(solution)/shard_map/ppermute | solution.py:10
  173.1 0.7 fusion.24
  175.8 0.2 conditional.13
  176.1 4.8 %collective-permute-start.6 = (f32[1024]{0:T(1024)S(1)}, f32[1024]{0:T(1024)S(1)}, u32[]{:S(2)}, u32[]{:S(2)}) collective-permute-start(f32[1024]{0:T(1024)S(1)} %max.73), channel_id=1, source_target_pairs={{2,0},{3,1},{4,2},{5,3},{6,4},{7,5},{8,6},{9,7},{10,8},{11,9},{12,... | collective-permute-start | bytes 12296 | tf_op jit(solution)/shard_map/ppermute | solution.py:10
  180.9 0.0 collective-permute-done.8
  180.9 1.3 fusion.15
  182.9 1.9 collective-permute-start.9
  184.9 11.5 %collective-permute-start.11 = (f32[512]{0:T(512)S(1)}, f32[512]{0:T(512)S(1)}, u32[]{:S(2)}, u32[]{:S(2)}) collective-permute-start(f32[512]{0:T(512)S(1)} %get-tuple-element.320), channel_id=1, source_target_pairs={{4,0},{5,1},{6,2},{7,3},{8,4},{9,5},{10,6},{11,7},{12,8},{13,9},{1... | collective-permute-start | bytes 6152 | tf_op jit(solution)/shard_map/ppermute | solution.py:10
  196.3 0.0 collective-permute-done.6
  196.4 1.9 collective-permute-start.14
  198.3 2.1 %collective-permute-start.15 = (f32[512]{0:T(512)S(1)}, f32[512]{0:T(512)S(1)}, u32[]{:S(2)}, u32[]{:S(2)}) collective-permute-start(f32[512]{0:T(512)S(1)} %get-tuple-element.328), channel_id=1, source_target_pairs={{0,4},{1,5},{2,6},{3,7},{4,8},{5,9},{6,10},{7,11},{8,12},{9,13},{1... | collective-permute-start | bytes 6152 | tf_op jit(solution)/shard_map/ppermute | solution.py:10
  200.5 5.3 %collective-permute-done.14 = f32[1024]{0:T(1024)S(1)} collective-permute-done((f32[1024]{0:T(1024)S(1)}, f32[1024]{0:T(1024)S(1)}, u32[]{:S(2)}, u32[]{:S(2)}) %collective-permute-start.14) | collective-permute-done | bytes 4128 | tf_op jit(solution)/shard_map/ppermute | solution.py:10
  205.8 2.8 %collective-permute-done.15 = f32[512]{0:T(512)S(1)} collective-permute-done((f32[512]{0:T(512)S(1)}, f32[512]{0:T(512)S(1)}, u32[]{:S(2)}, u32[]{:S(2)}) %collective-permute-start.15) | collective-permute-done | bytes 2080 | tf_op jit(solution)/shard_map/ppermute | solution.py:10
  208.6 0.6 broadcast_add_fusion
  (56 shorter events, 0.3 us)
Async XLA Ops:
  0.0 1.9 copy-start
  1.9 0.7 copy-start.4
  2.7 41.9 %collective-permute-start = (bf16[1040,768]{1,0:T(8,128)(2,1)S(1)}, bf16[1040,768]{1,0:T(8,128)(2,1)}, u32[]{:S(2)}, u32[]{:S(2)}) collective-permute-start(bf16[1040,768]{1,0:T(8,128)(2,1)S(1)} %fusion.13), channel_id=1, source_target_pairs={{1,0},{2,1},{3,2},{4,3},{5,4},{6,5},{7,6},{8,7},{9,8},{10,9},{11,1... | collective-permute-start | bytes 4792328 | tf_op jit(solution)/shard_map/ppermute | solution.py:10
  10.4 40.8 %collective-permute-start.1 = (bf16[1024,768]{1,0:T(8,128)(2,1)S(1)}, bf16[1024,768]{1,0:T(8,128)(2,1)S(1)}, u32[]{:S(2)}, u32[]{:S(2)}) collective-permute-start(bf16[1024,768]{1,0:T(8,128)(2,1)S(1)} %fusion.12), channel_id=1, source_target_pairs={{0,1},{1,2},{2,3},{3,4},{4,5},{5,6},{6,7},{7,8},{8,9},{9,10},{10,1... | collective-permute-start | bytes 4718600 | tf_op jit(solution)/shard_map/ppermute | solution.py:10
  44.6 40.2 %collective-permute-start.2 = (bf16[1040,768]{1,0:T(8,128)(2,1)}, bf16[1040,768]{1,0:T(8,128)(2,1)}, u32[]{:S(2)}, u32[]{:S(2)}) collective-permute-start(bf16[1040,768]{1,0:T(8,128)(2,1)} %collective-permute-done), channel_id=1, source_target_pairs={{1,0},{2,1},{3,2},{4,3},{5,4},{6,5},{7,6},{8,7},{9,8},{10,9},{11,1... | collective-permute-start | bytes 4792328 | tf_op jit(solution)/shard_map/ppermute | solution.py:10
  51.2 40.1 %copy-start.5 = (bf16[1024,768]{1,0:T(8,128)(2,1)}, bf16[1024,768]{1,0:T(8,128)(2,1)S(1)}, u32[]{:S(2)}) copy-start(bf16[1024,768]{1,0:T(8,128)(2,1)S(1)} %collective-permute-done.1) | copy-start | bytes 4718596
  51.2 40.1 %collective-permute-start.4 = (bf16[1024,768]{1,0:T(8,128)(2,1)S(1)}, bf16[1024,768]{1,0:T(8,128)(2,1)}, u32[]{:S(2)}, u32[]{:S(2)}) collective-permute-start(bf16[1024,768]{1,0:T(8,128)(2,1)S(1)} %collective-permute-done.1), channel_id=1, source_target_pairs={{0,1},{1,2},{2,3},{3,4},{4,5},{5,6},{6,7},{7,8},{8,9},{9,10},{10,1... | collective-permute-start | bytes 4718600 | tf_op jit(solution)/shard_map/ppermute | solution.py:10
  84.8 47.8 %collective-permute-start.5 = (bf16[1040,768]{1,0:T(8,128)(2,1)}, bf16[1040,768]{1,0:T(8,128)(2,1)S(1)}, u32[]{:S(2)}, u32[]{:S(2)}) collective-permute-start(bf16[1040,768]{1,0:T(8,128)(2,1)} %collective-permute-done.2), channel_id=1, source_target_pairs={{1,0},{2,1},{3,2},{4,3},{5,4},{6,5},{7,6},{8,7},{9,8},{10,9},{11,1... | collective-permute-start | bytes 4792328 | tf_op jit(solution)/shard_map/ppermute | solution.py:10
  91.3 38.4 %collective-permute-start.7 = (bf16[1024,768]{1,0:T(8,128)(2,1)}, bf16[1024,768]{1,0:T(8,128)(2,1)S(1)}, u32[]{:S(2)}, u32[]{:S(2)}) collective-permute-start(bf16[1024,768]{1,0:T(8,128)(2,1)} %collective-permute-done.4), channel_id=1, source_target_pairs={{0,1},{1,2},{2,3},{3,4},{4,5},{5,6},{6,7},{7,8},{8,9},{9,10},{10,1... | collective-permute-start | bytes 4718600 | tf_op jit(solution)/shard_map/ppermute | solution.py:10
  129.7 3.0 %copy-start.3 = (bf16[1024,768]{1,0:T(8,128)(2,1)}, bf16[1024,768]{1,0:T(8,128)(2,1)S(1)}, u32[]{:S(2)}) copy-start(bf16[1024,768]{1,0:T(8,128)(2,1)S(1)} %collective-permute-done.7) | copy-start | bytes 4718596
  130.7 45.4 %collective-permute-start.10 = (bf16[512,768]{1,0:T(8,128)(2,1)}, bf16[512,768]{1,0:T(8,128)(2,1)}, u32[]{:S(2)}, u32[]{:S(2)}) collective-permute-start(bf16[512,768]{1,0:T(8,128)(2,1)} %slice.170), channel_id=1, source_target_pairs={{0,1},{1,2},{2,3},{3,4},{4,5},{5,6},{6,7},{7,8},{8,9},{9,10},{10,1... | collective-permute-start | bytes 2359304 | tf_op jit(solution)/shard_map/ppermute | solution.py:10
  132.6 1.2 copy-start.1
  133.9 47.0 %collective-permute-start.8 = (bf16[528,768]{1,0:T(8,128)(2,1)S(1)}, bf16[528,768]{1,0:T(8,128)(2,1)}, u32[]{:S(2)}, u32[]{:S(2)}) collective-permute-start(bf16[528,768]{1,0:T(8,128)(2,1)S(1)} %pad_maximum_fusion), channel_id=1, source_target_pairs={{1,0},{2,1},{3,2},{4,3},{5,4},{6,5},{7,6},{8,7},{9,8},{10,9},{11,1... | collective-permute-start | bytes 2433032 | tf_op jit(solution)/shard_map/ppermute | solution.py:10
  152.4 48.1 %collective-permute-start.12 = (f32[1024]{0:T(1024)S(1)}, f32[1024]{0:T(1024)S(1)}, u32[]{:S(2)}, u32[]{:S(2)}) collective-permute-start(f32[1024]{0:T(1024)S(1)} %max.78), channel_id=1, source_target_pairs={{0,1},{1,2},{2,3},{3,4},{4,5},{5,6},{6,7},{7,8},{8,9},{9,10},{10,1... | collective-permute-start | bytes 12296 | tf_op jit(solution)/shard_map/ppermute | solution.py:10
  156.9 16.2 %copy-start.2 = (bf16[1040,768]{1,0:T(8,128)(2,1)S(1)}, bf16[1040,768]{1,0:T(8,128)(2,1)}, u32[]{:S(2)}) copy-start(bf16[1040,768]{1,0:T(8,128)(2,1)} %copy-done.1) | copy-start | bytes 4792324
  156.9 43.5 %collective-permute-start.13 = (f32[1024]{0:T(1024)S(1)}, f32[1024]{0:T(1024)S(1)}, u32[]{:S(2)}, u32[]{:S(2)}) collective-permute-start(f32[1024]{0:T(1024)S(1)} %max.80), channel_id=1, source_target_pairs={{0,2},{1,3},{2,4},{3,5},{4,6},{5,7},{6,8},{7,9},{8,10},{9,11},{10,... | collective-permute-start | bytes 12296 | tf_op jit(solution)/shard_map/ppermute | solution.py:10
  159.3 25.5 %collective-permute-start.3 = (f32[1024]{0:T(1024)S(1)}, f32[1024]{0:T(1024)S(1)}, u32[]{:S(2)}, u32[]{:S(2)}) collective-permute-start(f32[1024]{0:T(1024)S(1)} %max.71), channel_id=1, source_target_pairs={{1,0},{2,1},{3,2},{4,3},{5,4},{6,5},{7,6},{8,7},{9,8},{10,9},{11,1... | collective-permute-start | bytes 12296 | tf_op jit(solution)/shard_map/ppermute | solution.py:10
  176.1 20.3 %collective-permute-start.6 = (f32[1024]{0:T(1024)S(1)}, f32[1024]{0:T(1024)S(1)}, u32[]{:S(2)}, u32[]{:S(2)}) collective-permute-start(f32[1024]{0:T(1024)S(1)} %max.73), channel_id=1, source_target_pairs={{2,0},{3,1},{4,2},{5,3},{6,4},{7,5},{8,6},{9,7},{10,8},{11,9},{12,... | collective-permute-start | bytes 12296 | tf_op jit(solution)/shard_map/ppermute | solution.py:10
  182.9 15.4 %collective-permute-start.9 = (f32[1024]{0:T(1024)S(1)}, f32[1024]{0:T(1024)S(1)}, u32[]{:S(2)}, u32[]{:S(2)}) collective-permute-start(f32[1024]{0:T(1024)S(1)} %max.75), channel_id=1, source_target_pairs={{3,0},{4,1},{5,2},{6,3},{7,4},{8,5},{9,6},{10,7},{11,8},{12,9},{13... | collective-permute-start | bytes 12296 | tf_op jit(solution)/shard_map/ppermute | solution.py:10
  184.9 15.5 %collective-permute-start.11 = (f32[512]{0:T(512)S(1)}, f32[512]{0:T(512)S(1)}, u32[]{:S(2)}, u32[]{:S(2)}) collective-permute-start(f32[512]{0:T(512)S(1)} %get-tuple-element.320), channel_id=1, source_target_pairs={{4,0},{5,1},{6,2},{7,3},{8,4},{9,5},{10,6},{11,7},{12,8},{13,9},{1... | collective-permute-start | bytes 6152 | tf_op jit(solution)/shard_map/ppermute | solution.py:10
  196.4 9.4 %collective-permute-start.14 = (f32[1024]{0:T(1024)S(1)}, f32[1024]{0:T(1024)S(1)}, u32[]{:S(2)}, u32[]{:S(2)}) collective-permute-start(f32[1024]{0:T(1024)S(1)} %maximum_maximum_fusion), channel_id=1, source_target_pairs={{0,3},{1,4},{2,5},{3,6},{4,7},{5,8},{6,9},{7,10},{8,11},{9,12},{10... | collective-permute-start | bytes 12296 | tf_op jit(solution)/shard_map/ppermute | solution.py:10
  198.3 10.3 %collective-permute-start.15 = (f32[512]{0:T(512)S(1)}, f32[512]{0:T(512)S(1)}, u32[]{:S(2)}, u32[]{:S(2)}) collective-permute-start(f32[512]{0:T(512)S(1)} %get-tuple-element.328), channel_id=1, source_target_pairs={{0,4},{1,5},{2,6},{3,7},{4,8},{5,9},{6,10},{7,11},{8,12},{9,13},{1... | collective-permute-start | bytes 6152 | tf_op jit(solution)/shard_map/ppermute | solution.py:10
where the time goes:
time: 213 us; the launch traced here: 209 us
  waiting for transfers between devices  108 us (51%)
  starting transfers between devices  74.8 us (35%)
  matrix products  9.48 us (4%)
  other arithmetic  7.72 us (4%)
  between operations  5.62 us (3%)
  local copies, waits for them, and re-layouts  2.8 us (1%)
    ppermute x16, waiting for transfers between devices, from_behind(): lax.ppermute(value, axis, [(source, source + steps) for source in range(i...  108 us
    ppermute x16, starting transfers between devices, from_behind(): lax.ppermute(value, axis, [(source, source + steps) for source in range(i...  74.8 us
    dot_general x2, matrix products, compute(): sims = jnp.dot(a, b.T, preferred_element_type=jnp.float32)  7.43 us
  transfers between devices with their start and end apart: 16, of which 5 were waited for; matrix products, arithmetic and copies ran while one was open for 7% of the time, Pallas kernels for 0%

commit v1 on v0

--- a/solution.py
+++ b/solution.py
@@ -36,15 +36,6 @@
     meta = jnp.zeros((16, dim), jnp.bfloat16).at[0, :blocks].set(lag.astype(jnp.bfloat16))
     packet = jnp.concatenate([unit, meta], axis=0)
 
-    ahead = [packet]
-    for step in range(3):
-        ahead.append(from_behind(ahead[-1], "dev", -1))
-    ahead.append(from_behind(jnp.concatenate([ahead[3][: half * width], ahead[3][rows:]], axis=0), "dev", -1))
-    behind = [unit]
-    for step in range(3):
-        behind.append(from_behind(behind[-1], "dev", 1))
-    behind.append(from_behind(behind[3][half * width:], "dev", 1))
-
     def tile(i, a_blocks, j, b_count):
         a = behind[i]
         b = ahead[j]
@@ -72,13 +63,34 @@
     plan += [(3, everything, 4, half), (4, everything[half:], 3, blocks)]
     to_ahead = {}
     to_behind = {}
-    for i, a_blocks, j, b_count in plan:
-        row_part, column_part = tile(i, a_blocks, j, b_count)
-        if i == 0:
-            best = jnp.maximum(best, row_part)
+
+    def gather(pieces):
+        nonlocal best
+        for (i, a_blocks, j, b_count), (row_part, column_part) in pieces:
+            if i == 0:
+                best = jnp.maximum(best, row_part)
+            else:
+                to_behind[i] = jnp.maximum(to_behind[i], row_part) if i in to_behind else row_part
+            to_ahead[j] = jnp.maximum(to_ahead[j], column_part) if j in to_ahead else column_part
+
+    ahead = [packet]
+    behind = [unit]
+    hops = 4
+    for hop in range(1, hops + 1):
+        if hop < hops:
+            a_next = from_behind(ahead[-1], "dev", -1)
+            b_next = from_behind(behind[-1], "dev", 1)
         else:
-            to_behind[i] = jnp.maximum(to_behind[i], row_part) if i in to_behind else row_part
-        to_ahead[j] = jnp.maximum(to_ahead[j], column_part) if j in to_ahead else column_part
+            a_next = from_behind(jnp.concatenate([ahead[-1][: half * width], ahead[-1][rows:]], axis=0), "dev", -1)
+            b_next = from_behind(behind[-1][half * width:], "dev", 1)
+        ready = [entry for entry in plan if max(entry[0], entry[2]) == hop - 1]
+        pieces = [tile(*entry) for entry in ready]
+        a_next, b_next, best, pieces = lax.optimization_barrier((a_next, b_next, best, pieces))
+        gather(zip(ready, pieces))
+        ahead.append(a_next)
+        behind.append(b_next)
+    ready = [entry for entry in plan if max(entry[0], entry[2]) == hops]
+    gather(zip(ready, [tile(*entry) for entry in ready]))
 
     for i, part in to_behind.items():
         arrived = from_behind(part, "dev", -i)

time: 213 us -> 193 us (0.906)
  the two profiles are of different devices: /device:TPU:4 before, /device:TPU:74 now
where the time goes in v1:
time: 193 us
  waiting for transfers between devices  107 us (55%)
  starting transfers between devices  63.8 us (33%)
  other arithmetic  7.88 us (4%)
  between operations  5.7 us (3%)
  matrix products  5.53 us (3%)
  local copies, waits for them, and re-layouts  2.85 us (1%)
    ppermute x16, waiting for transfers between devices, from_behind(): lax.ppermute(value, axis, [(source, source + steps) for source in range(i...  107 us
    ppermute x16, starting transfers between devices, from_behind(): lax.ppermute(value, axis, [(source, source + steps) for source in range(i...  63.8 us
  transfers between devices with their start and end apart: 16, of which 6 were waited for; matrix products, arithmetic and copies ran while one was open for 6% of the time, Pallas kernels for 0%

profile of v1, /device:TPU:74, one launch (start us, length us, event | category | flops | bytes accessed | tf_op | source)
XLA Modules:
  0.0 193.1 jit_solution(6589383574997422467)
XLA Ops:
  0.0 1.9 fusion.11
  1.9 0.0 copy-start.3
  1.9 0.3 fusion.12
  2.3 0.3 copy-done.3
  2.6 0.1 fusion.13
  2.7 2.0 %collective-permute-start = (bf16[1040,768]{1,0:T(8,128)(2,1)S(1)}, bf16[1040,768]{1,0:T(8,128)(2,1)}, u32[]{:S(2)}, u32[]{:S(2)}) collective-permute-start(bf16[1040,768]{1,0:T(8,128)(2,1)S(1)} %fusion.13), channel_id=1, source_target_pairs={{1,0},{2,1},{3,2},{4,3},{5,4},{6,5},{7,6},{8,7},{9,8},{10,9},{11,1... | collective-permute-start | bytes 4792328 | tf_op jit(solution)/shard_map/ppermute | solution.py:10
  4.7 3.8 %collective-permute-start.1 = (bf16[1024,768]{1,0:T(8,128)(2,1)S(1)}, bf16[1024,768]{1,0:T(8,128)(2,1)}, u32[]{:S(2)}, u32[]{:S(2)}) collective-permute-start(bf16[1024,768]{1,0:T(8,128)(2,1)S(1)} %fusion.12), channel_id=1, source_target_pairs={{0,1},{1,2},{2,3},{3,4},{4,5},{5,6},{6,7},{7,8},{8,9},{9,10},{10,1... | collective-permute-start | bytes 4718600 | tf_op jit(solution)/shard_map/ppermute | solution.py:10
  8.5 0.1 broadcast_bitcast_fusion.16
  8.6 2.1 %select_reduce_fusion = f32[1024]{0:T(1024)S(1)} fusion(s32[1024]{0:T(1024)S(1)} %bitcast.118, bf16[1024,768]{1,0:T(8,128)(2,1)S(1)} %fusion.12), kind=kOutput, calls=%fused_computation.33 | convolution fusion | flops 1616903168 | bytes 1581056 | tf_op jit(solution)/shard_map/dot_general | solution.py:31
  10.7 32.1 %collective-permute-done.1 = bf16[1024,768]{1,0:T(8,128)(2,1)} collective-permute-done((bf16[1024,768]{1,0:T(8,128)(2,1)S(1)}, bf16[1024,768]{1,0:T(8,128)(2,1)}, u32[]{:S(2)}, u32[]{:S(2)}) %collective-permute-start.1) | collective-permute-done | bytes 1572896 | tf_op jit(solution)/shard_map/ppermute | solution.py:10
  42.7 0.0 collective-permute-done
  42.8 5.9 %collective-permute-start.2 = (bf16[1040,768]{1,0:T(8,128)(2,1)}, bf16[1040,768]{1,0:T(8,128)(2,1)}, u32[]{:S(2)}, u32[]{:S(2)}) collective-permute-start(bf16[1040,768]{1,0:T(8,128)(2,1)} %collective-permute-done), channel_id=1, source_target_pairs={{1,0},{2,1},{3,2},{4,3},{5,4},{6,5},{7,6},{8,7},{9,8},{10,9},{11,1... | collective-permute-start | bytes 4792328 | tf_op jit(solution)/shard_map/ppermute | solution.py:10
  48.7 1.9 collective-permute-start.3
  50.6 1.4 fusion.15
  53.4 3.6 %conditional.8 = (f32[1024]{0:T(1024)S(1)}, f32[1024]{0:T(1024)S(1)}) conditional(s32[]{:T(128)} %convert_element_type.66, () %tuple.128, (s32[4]{0:T(128)S(1)}, s32[4]{0:T(128)S(1)}, bf16[1024,768]{1,0:T(8,128)(2,1)S(1)}, bf16[1040,768]{1,0:T(8,128)(2,1)}) %tuple.129), branch_computations={%region_3.4_spmd, %region_4.7_spmd} | conditional | flops 1641101312 | bytes 3227892 | solution.py:59
  53.4 0.1 broadcast_bitcast_fusion
  53.5 3.5 %fusion.22 = (f32[1040]{0:T(1024)S(1)}, f32[1024]{0:T(1024)S(1)}) fusion(bf16[1024,768]{1,0:T(8,128)(2,1)S(1)} %get-tuple-element.267, bf16[1040,768]{1,0:T(8,128)(2,1)} %get-tuple-element.268, s32[1024]{0:T(1024)S(1)} %bitcast.113, s32[1040]{0:T(1024)S(1)} %concatenate.38), kind=kOutput, calls=%fused_computation.69 | convolution fusion | flops 1641101312 | bytes 3186816 | tf_op jit(solution)/shard_map/cond/branch_1_fun/dot_general | solution.py:51
  57.0 30.6 %collective-permute-done.3 = bf16[1024,768]{1,0:T(8,128)(2,1)S(1)} collective-permute-done((bf16[1024,768]{1,0:T(8,128)(2,1)}, bf16[1024,768]{1,0:T(8,128)(2,1)S(1)}, u32[]{:S(2)}, u32[]{:S(2)}) %collective-permute-start.3) | collective-permute-done | bytes 1572896 | tf_op jit(solution)/shard_map/ppermute | solution.py:10
  87.6 0.0 collective-permute-done.2
  87.6 1.1 copy-done.4
  88.8 3.6 %collective-permute-start.4 = (bf16[1040,768]{1,0:T(8,128)(2,1)}, bf16[1040,768]{1,0:T(8,128)(2,1)S(1)}, u32[]{:S(2)}, u32[]{:S(2)}) collective-permute-start(bf16[1040,768]{1,0:T(8,128)(2,1)} %collective-permute-done.2), channel_id=1, source_target_pairs={{1,0},{2,1},{3,2},{4,3},{5,4},{6,5},{7,6},{8,7},{9,8},{10,9},{11,1... | collective-permute-start | bytes 4792328 | tf_op jit(solution)/shard_map/ppermute | solution.py:10
  92.4 2.2 %collective-permute-start.5 = (bf16[1024,768]{1,0:T(8,128)(2,1)}, bf16[1024,768]{1,0:T(8,128)(2,1)S(1)}, u32[]{:S(2)}, u32[]{:S(2)}) collective-permute-start(bf16[1024,768]{1,0:T(8,128)(2,1)} %copy-done.4), channel_id=1, source_target_pairs={{0,1},{1,2},{2,3},{3,4},{4,5},{5,6},{6,7},{7,8},{8,9},{9,10},{10,1... | collective-permute-start | bytes 4718600 | tf_op jit(solution)/shard_map/ppermute | solution.py:10
  94.6 1.4 fusion.17
  97.4 31.6 %collective-permute-done.5 = bf16[1024,768]{1,0:T(8,128)(2,1)S(1)} collective-permute-done((bf16[1024,768]{1,0:T(8,128)(2,1)}, bf16[1024,768]{1,0:T(8,128)(2,1)S(1)}, u32[]{:S(2)}, u32[]{:S(2)}) %collective-permute-start.5) | collective-permute-done | bytes 1572896 | tf_op jit(solution)/shard_map/ppermute | solution.py:10
  129.0 0.1 slice.149
  129.1 1.1 copy-done.1
  130.2 0.1 pad_maximum_fusion
  130.2 3.8 %collective-permute-start.6 = (bf16[528,768]{1,0:T(8,128)(2,1)S(1)}, bf16[528,768]{1,0:T(8,128)(2,1)}, u32[]{:S(2)}, u32[]{:S(2)}) collective-permute-start(bf16[528,768]{1,0:T(8,128)(2,1)S(1)} %pad_maximum_fusion), channel_id=1, source_target_pairs={{1,0},{2,1},{3,2},{4,3},{5,4},{6,5},{7,6},{8,7},{9,8},{10,9},{11,1... | collective-permute-start | bytes 2433032 | tf_op jit(solution)/shard_map/ppermute | solution.py:10
  134.0 0.1 slice.151
  134.1 2.2 %collective-permute-start.7 = (bf16[512,768]{1,0:T(8,128)(2,1)S(1)}, bf16[512,768]{1,0:T(8,128)(2,1)}, u32[]{:S(2)}, u32[]{:S(2)}) collective-permute-start(bf16[512,768]{1,0:T(8,128)(2,1)S(1)} %slice.151), channel_id=1, source_target_pairs={{0,1},{1,2},{2,3},{3,4},{4,5},{5,6},{6,7},{7,8},{8,9},{9,10},{10,1... | collective-permute-start | bytes 2359304 | tf_op jit(solution)/shard_map/ppermute | solution.py:10
  136.3 2.7 %collective-permute-start.12 = (f32[1024]{0:T(1024)S(1)}, f32[1024]{0:T(1024)S(1)}, u32[]{:S(2)}, u32[]{:S(2)}) collective-permute-start(f32[1024]{0:T(1024)S(1)} %max.78), channel_id=1, source_target_pairs={{0,1},{1,2},{2,3},{3,4},{4,5},{5,6},{6,7},{7,8},{8,9},{9,10},{10,1... | collective-permute-start | bytes 12296 | tf_op jit(solution)/shard_map/ppermute | solution.py:10
  139.1 3.2 %collective-permute-start.8 = (f32[1024]{0:T(1024)S(1)}, f32[1024]{0:T(1024)S(1)}, u32[]{:S(2)}, u32[]{:S(2)}) collective-permute-start(f32[1024]{0:T(1024)S(1)} %max.71), channel_id=1, source_target_pairs={{1,0},{2,1},{3,2},{4,3},{5,4},{6,5},{7,6},{8,7},{9,8},{10,9},{11,1... | collective-permute-start | bytes 12296 | tf_op jit(solution)/shard_map/ppermute | solution.py:10
  142.3 0.7 fusion.19
  144.9 3.6 %collective-permute-start.13 = (f32[1024]{0:T(1024)S(1)}, f32[1024]{0:T(1024)S(1)}, u32[]{:S(2)}, u32[]{:S(2)}) collective-permute-start(f32[1024]{0:T(1024)S(1)} %max.80), channel_id=1, source_target_pairs={{0,2},{1,3},{2,4},{3,5},{4,6},{5,7},{6,8},{7,9},{8,10},{9,11},{10,... | collective-permute-start | bytes 12296 | tf_op jit(solution)/shard_map/ppermute | solution.py:10
  148.5 0.2 conditional.12
  148.8 4.3 %collective-permute-done.7 = bf16[512,768]{1,0:T(8,128)(2,1)} collective-permute-done((bf16[512,768]{1,0:T(8,128)(2,1)S(1)}, bf16[512,768]{1,0:T(8,128)(2,1)}, u32[]{:S(2)}, u32[]{:S(2)}) %collective-permute-start.7) | collective-permute-done | bytes 786464 | tf_op jit(solution)/shard_map/ppermute | solution.py:10
  153.1 5.5 %collective-permute-start.9 = (f32[1024]{0:T(1024)S(1)}, f32[1024]{0:T(1024)S(1)}, u32[]{:S(2)}, u32[]{:S(2)}) collective-permute-start(f32[1024]{0:T(1024)S(1)} %max.73), channel_id=1, source_target_pairs={{2,0},{3,1},{4,2},{5,3},{6,4},{7,5},{8,6},{9,7},{10,8},{11,9},{12,... | collective-permute-start | bytes 12296 | tf_op jit(solution)/shard_map/ppermute | solution.py:10
  158.5 1.4 convert_subtract_fusion
  160.7 6.1 %collective-permute-start.10 = (f32[1024]{0:T(1024)S(1)}, f32[1024]{0:T(1024)S(1)}, u32[]{:S(2)}, u32[]{:S(2)}) collective-permute-start(f32[1024]{0:T(1024)S(1)} %max.75), channel_id=1, source_target_pairs={{3,0},{4,1},{5,2},{6,3},{7,4},{8,5},{9,6},{10,7},{11,8},{12,9},{13... | collective-permute-start | bytes 12296 | tf_op jit(solution)/shard_map/ppermute | solution.py:10
  166.8 0.0 collective-permute-done.8
  166.8 8.4 %collective-permute-start.11 = (f32[512]{0:T(512)S(1)}, f32[512]{0:T(512)S(1)}, u32[]{:S(2)}, u32[]{:S(2)}) collective-permute-start(f32[512]{0:T(512)S(1)} %get-tuple-element.368), channel_id=1, source_target_pairs={{4,0},{5,1},{6,2},{7,3},{8,4},{9,5},{10,6},{11,7},{12,8},{13,9},{1... | collective-permute-start | bytes 6152 | tf_op jit(solution)/shard_map/ppermute | solution.py:10
  175.2 0.0 collective-permute-done.9
  175.3 6.9 %collective-permute-start.14 = (f32[1024]{0:T(1024)S(1)}, f32[1024]{0:T(1024)S(1)}, u32[]{:S(2)}, u32[]{:S(2)}) collective-permute-start(f32[1024]{0:T(1024)S(1)} %maximum_maximum_fusion), channel_id=1, source_target_pairs={{0,3},{1,4},{2,5},{3,6},{4,7},{5,8},{6,9},{7,10},{8,11},{9,12},{10... | collective-permute-start | bytes 12296 | tf_op jit(solution)/shard_map/ppermute | solution.py:10
  182.2 0.0 collective-permute-done.10
  182.2 1.9 collective-permute-start.15
  184.2 0.5 collective-permute-done.14
  184.7 7.8 %collective-permute-done.15 = f32[512]{0:T(512)S(1)} collective-permute-done((f32[512]{0:T(512)S(1)}, f32[512]{0:T(512)S(1)}, u32[]{:S(2)}, u32[]{:S(2)}) %collective-permute-start.15) | collective-permute-done | bytes 2080 | tf_op jit(solution)/shard_map/ppermute | solution.py:10
  192.5 0.6 broadcast_add_fusion
  (51 shorter events, 0.4 us)
Async XLA Ops:
  0.0 1.9 %copy-start = (bf16[1024,768]{1,0:T(8,128)(2,1)S(1)}, bf16[1024,768]{1,0:T(8,128)(2,1)}, u32[]{:S(2)}) copy-start(bf16[1024,768]{1,0:T(8,128)(2,1)} %param.56) | copy-start | bytes 4718596
  1.9 0.7 copy-start.3
  2.7 40.1 %collective-permute-start = (bf16[1040,768]{1,0:T(8,128)(2,1)S(1)}, bf16[1040,768]{1,0:T(8,128)(2,1)}, u32[]{:S(2)}, u32[]{:S(2)}) collective-permute-start(bf16[1040,768]{1,0:T(8,128)(2,1)S(1)} %fusion.13), channel_id=1, source_target_pairs={{1,0},{2,1},{3,2},{4,3},{5,4},{6,5},{7,6},{8,7},{9,8},{10,9},{11,1... | collective-permute-start | bytes 4792328 | tf_op jit(solution)/shard_map/ppermute | solution.py:10
  4.7 38.0 %collective-permute-start.1 = (bf16[1024,768]{1,0:T(8,128)(2,1)S(1)}, bf16[1024,768]{1,0:T(8,128)(2,1)}, u32[]{:S(2)}, u32[]{:S(2)}) collective-permute-start(bf16[1024,768]{1,0:T(8,128)(2,1)S(1)} %fusion.12), channel_id=1, source_target_pairs={{0,1},{1,2},{2,3},{3,4},{4,5},{5,6},{6,7},{7,8},{8,9},{9,10},{10,1... | collective-permute-start | bytes 4718600 | tf_op jit(solution)/shard_map/ppermute | solution.py:10
  42.8 44.9 %collective-permute-start.2 = (bf16[1040,768]{1,0:T(8,128)(2,1)}, bf16[1040,768]{1,0:T(8,128)(2,1)}, u32[]{:S(2)}, u32[]{:S(2)}) collective-permute-start(bf16[1040,768]{1,0:T(8,128)(2,1)} %collective-permute-done), channel_id=1, source_target_pairs={{1,0},{2,1},{3,2},{4,3},{5,4},{6,5},{7,6},{8,7},{9,8},{10,9},{11,1... | collective-permute-start | bytes 4792328 | tf_op jit(solution)/shard_map/ppermute | solution.py:10
  48.7 38.9 %collective-permute-start.3 = (bf16[1024,768]{1,0:T(8,128)(2,1)}, bf16[1024,768]{1,0:T(8,128)(2,1)S(1)}, u32[]{:S(2)}, u32[]{:S(2)}) collective-permute-start(bf16[1024,768]{1,0:T(8,128)(2,1)} %collective-permute-done.1), channel_id=1, source_target_pairs={{0,1},{1,2},{2,3},{3,4},{4,5},{5,6},{6,7},{7,8},{8,9},{9,10},{10,1... | collective-permute-start | bytes 4718600 | tf_op jit(solution)/shard_map/ppermute | solution.py:10
  87.6 1.2 copy-start.4
  88.8 40.3 %collective-permute-start.4 = (bf16[1040,768]{1,0:T(8,128)(2,1)}, bf16[1040,768]{1,0:T(8,128)(2,1)S(1)}, u32[]{:S(2)}, u32[]{:S(2)}) collective-permute-start(bf16[1040,768]{1,0:T(8,128)(2,1)} %collective-permute-done.2), channel_id=1, source_target_pairs={{1,0},{2,1},{3,2},{4,3},{5,4},{6,5},{7,6},{8,7},{9,8},{10,9},{11,1... | collective-permute-start | bytes 4792328 | tf_op jit(solution)/shard_map/ppermute | solution.py:10
  92.4 36.6 %collective-permute-start.5 = (bf16[1024,768]{1,0:T(8,128)(2,1)}, bf16[1024,768]{1,0:T(8,128)(2,1)S(1)}, u32[]{:S(2)}, u32[]{:S(2)}) collective-permute-start(bf16[1024,768]{1,0:T(8,128)(2,1)} %copy-done.4), channel_id=1, source_target_pairs={{0,1},{1,2},{2,3},{3,4},{4,5},{5,6},{6,7},{7,8},{8,9},{9,10},{10,1... | collective-permute-start | bytes 4718600 | tf_op jit(solution)/shard_map/ppermute | solution.py:10
  129.0 1.1 copy-start.1
  130.2 3.8 %copy-start.2 = (bf16[1024,768]{1,0:T(8,128)(2,1)S(1)}, bf16[1024,768]{1,0:T(8,128)(2,1)}, u32[]{:S(2)}) copy-start(bf16[1024,768]{1,0:T(8,128)(2,1)} %copy-done.1) | copy-start | bytes 4718596
  130.2 22.8 %collective-permute-start.6 = (bf16[528,768]{1,0:T(8,128)(2,1)S(1)}, bf16[528,768]{1,0:T(8,128)(2,1)}, u32[]{:S(2)}, u32[]{:S(2)}) collective-permute-start(bf16[528,768]{1,0:T(8,128)(2,1)S(1)} %pad_maximum_fusion), channel_id=1, source_target_pairs={{1,0},{2,1},{3,2},{4,3},{5,4},{6,5},{7,6},{8,7},{9,8},{10,9},{11,1... | collective-permute-start | bytes 2433032 | tf_op jit(solution)/shard_map/ppermute | solution.py:10
  134.1 19.0 %collective-permute-start.7 = (bf16[512,768]{1,0:T(8,128)(2,1)S(1)}, bf16[512,768]{1,0:T(8,128)(2,1)}, u32[]{:S(2)}, u32[]{:S(2)}) collective-permute-start(bf16[512,768]{1,0:T(8,128)(2,1)S(1)} %slice.151), channel_id=1, source_target_pairs={{0,1},{1,2},{2,3},{3,4},{4,5},{5,6},{6,7},{7,8},{8,9},{9,10},{10,1... | collective-permute-start | bytes 2359304 | tf_op jit(solution)/shard_map/ppermute | solution.py:10
  136.3 47.8 %collective-permute-start.12 = (f32[1024]{0:T(1024)S(1)}, f32[1024]{0:T(1024)S(1)}, u32[]{:S(2)}, u32[]{:S(2)}) collective-permute-start(f32[1024]{0:T(1024)S(1)} %max.78), channel_id=1, source_target_pairs={{0,1},{1,2},{2,3},{3,4},{4,5},{5,6},{6,7},{7,8},{8,9},{9,10},{10,1... | collective-permute-start | bytes 12296 | tf_op jit(solution)/shard_map/ppermute | solution.py:10
  139.1 27.7 %collective-permute-start.8 = (f32[1024]{0:T(1024)S(1)}, f32[1024]{0:T(1024)S(1)}, u32[]{:S(2)}, u32[]{:S(2)}) collective-permute-start(f32[1024]{0:T(1024)S(1)} %max.71), channel_id=1, source_target_pairs={{1,0},{2,1},{3,2},{4,3},{5,4},{6,5},{7,6},{8,7},{9,8},{10,9},{11,1... | collective-permute-start | bytes 12296 | tf_op jit(solution)/shard_map/ppermute | solution.py:10
  144.9 39.3 %collective-permute-start.13 = (f32[1024]{0:T(1024)S(1)}, f32[1024]{0:T(1024)S(1)}, u32[]{:S(2)}, u32[]{:S(2)}) collective-permute-start(f32[1024]{0:T(1024)S(1)} %max.80), channel_id=1, source_target_pairs={{0,2},{1,3},{2,4},{3,5},{4,6},{5,7},{6,8},{7,9},{8,10},{9,11},{10,... | collective-permute-start | bytes 12296 | tf_op jit(solution)/shard_map/ppermute | solution.py:10
  153.1 22.2 %collective-permute-start.9 = (f32[1024]{0:T(1024)S(1)}, f32[1024]{0:T(1024)S(1)}, u32[]{:S(2)}, u32[]{:S(2)}) collective-permute-start(f32[1024]{0:T(1024)S(1)} %max.73), channel_id=1, source_target_pairs={{2,0},{3,1},{4,2},{5,3},{6,4},{7,5},{8,6},{9,7},{10,8},{11,9},{12,... | collective-permute-start | bytes 12296 | tf_op jit(solution)/shard_map/ppermute | solution.py:10
  160.7 21.5 %collective-permute-start.10 = (f32[1024]{0:T(1024)S(1)}, f32[1024]{0:T(1024)S(1)}, u32[]{:S(2)}, u32[]{:S(2)}) collective-permute-start(f32[1024]{0:T(1024)S(1)} %max.75), channel_id=1, source_target_pairs={{3,0},{4,1},{5,2},{6,3},{7,4},{8,5},{9,6},{10,7},{11,8},{12,9},{13... | collective-permute-start | bytes 12296 | tf_op jit(solution)/shard_map/ppermute | solution.py:10
  166.8 17.3 %collective-permute-start.11 = (f32[512]{0:T(512)S(1)}, f32[512]{0:T(512)S(1)}, u32[]{:S(2)}, u32[]{:S(2)}) collective-permute-start(f32[512]{0:T(512)S(1)} %get-tuple-element.368), channel_id=1, source_target_pairs={{4,0},{5,1},{6,2},{7,3},{8,4},{9,5},{10,6},{11,7},{12,8},{13,9},{1... | collective-permute-start | bytes 6152 | tf_op jit(solution)/shard_map/ppermute | solution.py:10
  175.3 9.5 %collective-permute-start.14 = (f32[1024]{0:T(1024)S(1)}, f32[1024]{0:T(1024)S(1)}, u32[]{:S(2)}, u32[]{:S(2)}) collective-permute-start(f32[1024]{0:T(1024)S(1)} %maximum_maximum_fusion), channel_id=1, source_target_pairs={{0,3},{1,4},{2,5},{3,6},{4,7},{5,8},{6,9},{7,10},{8,11},{9,12},{10... | collective-permute-start | bytes 12296 | tf_op jit(solution)/shard_map/ppermute | solution.py:10
  182.2 10.3 %collective-permute-start.15 = (f32[512]{0:T(512)S(1)}, f32[512]{0:T(512)S(1)}, u32[]{:S(2)}, u32[]{:S(2)}) collective-permute-start(f32[512]{0:T(512)S(1)} %get-tuple-element.376), channel_id=1, source_target_pairs={{0,4},{1,5},{2,6},{3,7},{4,8},{5,9},{6,10},{7,11},{8,12},{9,13},{1... | collective-permute-start | bytes 6152 | tf_op jit(solution)/shard_map/ppermute | solution.py:10
